TPU v7x, 256 devices: a whole 4x4x8 slice. The times are simulated.
256 devices in a mesh: gx: 32 (over x, y, core), gy: 8 (over z).
Axes of the slice: x: 4, y: 4, z: 8, core: 2. Of those that a mesh axis runs over, the one named last changes fastest.
Arguments:
- orbitals: float32 [64, 128, 64, 128], P(None, 'gx', 'gy'), may hold values from -60 to 60, as said below
- potential: float32 [128, 64, 128], P('gx', 'gy'), may hold values from 0.2 to 2
Outputs:
- basis: float32 [64, 128, 64, 128], P(None, 'gx', 'gy')
- factor: float32 [64, 64], replicated
Inputs may be any that keep to these rules, and one draw needn't show every extreme that they name: `orbitals`: Real-valued entries.
All inputs are finite; a program needn't handle non-finite values.
Results may differ from a plain program's by a relative error of at most 0.00011.
Values sent between devices are 32-bit elements; how exact they have to be, the bound alone decides.
No kernel may reach another device: no remote copies, remote signals or barrier semaphores. Data moves between devices by JAX's collectives and lax.ppermute only.
A program may use at most 64 MiB of HBM per device.

v0:
```python
import jax
import jax.numpy as jnp
from jax import lax
from jax.sharding import PartitionSpec as P


def extended(cells, sides, width):
    for axis, dim in sides:
        count = lax.axis_size(axis)
        head = lax.slice_in_dim(cells, 0, width, axis=dim)
        tail = lax.slice_in_dim(cells, cells.shape[dim] - width, cells.shape[dim], axis=dim)
        cells = jnp.concatenate(
            [
                lax.ppermute(tail, axis, [(i, (i + 1) % count) for i in range(count)]),
                cells,
                lax.ppermute(head, axis, [((i + 1) % count, i) for i in range(count)]),
            ],
            axis=dim,
        )
    return cells


def apply_ham(padded, pot):
    core = padded[:, 2:-2, 2:-2]
    total = -7.5 * core
    total = total + 4.0 / 3.0 * (padded[:, 3:-1, 2:-2] + padded[:, 1:-3, 2:-2])
    total = total - 1.0 / 12.0 * (padded[:, 4:, 2:-2] + padded[:, :-4, 2:-2])
    total = total + 4.0 / 3.0 * (padded[:, 2:-2, 3:-1] + padded[:, 2:-2, 1:-3])
    total = total - 1.0 / 12.0 * (padded[:, 2:-2, 4:] + padded[:, 2:-2, :-4])
    total = total + 4.0 / 3.0 * (jnp.roll(core, 1, 3) + jnp.roll(core, -1, 3))
    total = total - 1.0 / 12.0 * (jnp.roll(core, 2, 3) + jnp.roll(core, -2, 3))
    return -0.5 * total + pot[None] * core


def with_faces(field):
    return extended(field, (("gx", 1), ("gy", 2)), 2)


def upper_factor(gram):
    order = gram.shape[0]
    index = jnp.arange(order)

    def column_step(col, lower):
        row_now = lax.dynamic_slice_in_dim(lower, col, 1, 0)[0]
        target = lax.dynamic_slice_in_dim(gram, col, 1, 1)[:, 0]
        column = target - jnp.dot(
            lower, row_now, precision=lax.Precision.HIGHEST, preferred_element_type=jnp.float32
        )
        pivot = jnp.sqrt(jnp.sum(jnp.where(index == col, column, 0.0)))
        values = jnp.where(index == col, pivot, column / pivot)
        values = jnp.where(index >= col, values, 0.0)
        return jnp.where(index[None, :] == col, values[:, None], lower)

    lower = lax.fori_loop(0, order, column_step, jnp.zeros_like(gram))
    return lower.T


def upper_inverse(upper):
    order = upper.shape[0]
    index = jnp.arange(order)

    def row_step(step, inverse):
        row = order - 1 - step
        upper_row = lax.dynamic_slice_in_dim(upper, row, 1, 0)[0]
        pivot = jnp.sum(jnp.where(index == row, upper_row, 0.0))
        rest = jnp.dot(
            upper_row, inverse, precision=lax.Precision.HIGHEST, preferred_element_type=jnp.float32
        )
        unit = jnp.where(index == row, 1.0, 0.0).astype(jnp.float32)
        new_row = (unit - rest) / pivot
        return jnp.where(index[:, None] == row, new_row[None, :], inverse)

    return lax.fori_loop(0, order, row_step, jnp.zeros_like(upper))


def shards(orbitals, potential):
    first = (apply_ham(with_faces(orbitals), potential) - 5.5 * orbitals) / 4.5
    applied = apply_ham(with_faces(first), potential)
    filtered = 2.0 * (applied - 5.5 * first) / 4.5 - orbitals
    width = filtered.shape[0]
    flat = filtered.reshape(width, -1)
    cells = flat.shape[1] * lax.axis_size("gx") * lax.axis_size("gy")
    local_gram = (
        jnp.dot(flat, flat.T, precision=lax.Precision.HIGHEST, preferred_element_type=jnp.float32)
        / cells
    )
    factor = upper_factor(lax.psum(local_gram, ("gx", "gy")))
    inverse = upper_inverse(factor)
    solved = jnp.dot(
        inverse.T, flat, precision=lax.Precision.HIGHEST, preferred_element_type=jnp.float32
    )
    basis = (solved * jnp.sqrt(jnp.float32(cells))).reshape(filtered.shape)
    return (basis, factor)


def solution(mesh):
    return jax.shard_map(
        shards,
        mesh=mesh,
        in_specs=(P(None, "gx", "gy", None), P("gx", "gy", None)),
        out_specs=(P(None, "gx", "gy", None), P()),
        check_vma=False,
    )
```

profile of v0, /device:TPU:1, one launch (start us, length us, event | category | flops | bytes accessed | tf_op | source)
XLA Modules:
  0.0 353.4 jit_solution(158170441676691293)
XLA Ops:
  0.6 2.4 fusion.60
  3.0 3.2 collective-permute-start
  8.3 4.5 %collective-permute-done = f32[64,2,8,128]{3,2,1,0:T(8,128)S(1)} collective-permute-done((f32[64,2,8,128]{3,2,1,0:T(8,128)}, f32[64,2,8,128]{3,2,1,0:T(8,128)S(1)}, u32[]{:S(2)}, u32[]{:S(2)}) %collective-permute-start) | collective-permute-done | bytes 524320 | tf_op jit(solution)/shard_map/ppermute | solution.py:16
  13.7 5.7 %collective-permute-start.2 = (f32[64,8,2,128]{3,1,2,0:T(8,128)S(1)}, f32[64,8,2,128]{3,1,2,0:T(8,128)S(1)}, u32[]{:S(2)}, u32[]{:S(2)}) collective-permute-start(f32[64,8,2,128]{3,1,2,0:T(8,128)S(1)} %get-tuple-element.266), channel_id=1, source_target_pairs={{1,0},{2,1},{3,2},{4,3},{5,4},{6,5},{7,6},{0,7},{9,8},{10,9},{11,1... | collective-permute-start | bytes 1572872 | tf_op jit(solution)/shard_map/ppermute | solution.py:16
  20.6 4.8 %collective-permute-done.2 = f32[64,8,2,128]{3,1,2,0:T(8,128)S(1)} collective-permute-done((f32[64,8,2,128]{3,1,2,0:T(8,128)S(1)}, f32[64,8,2,128]{3,1,2,0:T(8,128)S(1)}, u32[]{:S(2)}, u32[]{:S(2)}) %collective-permute-start.2) | collective-permute-done | bytes 524320 | tf_op jit(solution)/shard_map/ppermute | solution.py:16
  25.4 3.1 collective-permute-done.3
  28.6 7.3 %broadcast_multiply_fusion = (f32[64,4,8,128]{3,1,2,0:T(4,128)S(1)}, f32[64,4,8,128]{3,1,2,0:T(4,128)S(1)}) fusion(f32[64,4,8,128]{3,1,2,0:T(4,128)S(1)} %copy.55, f32[4,8,128]{2,0,1:T(4,128)S(1)} %copy.71, f32[64,4,8,2]{3,1,2,0:T(4,128)S(1)} %get-tuple-element.285, f32[64,4,8,126]{3,1,2,0:T(4,128)S(1)} %get-tuple-element.287, ...), kind=kLoop, calls=%fused_computation.105 | loop fusion | flops 11796480 | bytes 9453568 | tf_op jit(solution)/shard_map/div | solution.py:77
  36.4 9.8 %collective-permute-start.4 = (f32[64,2,8,128]{3,2,1,0:T(8,128)S(1)}, f32[64,2,8,128]{3,2,1,0:T(8,128)S(1)}, u32[]{:S(2)}, u32[]{:S(2)}) collective-permute-start(f32[64,2,8,128]{3,2,1,0:T(8,128)S(1)} %copy.74), channel_id=1, source_target_pairs={{8,0},{16,8},{24,16},{32,24},{40,32},{48,40},{56,48},{64,56},{72,6... | collective-permute-start | bytes 1572872 | tf_op jit(solution)/shard_map/ppermute | solution.py:16
  47.7 3.3 collective-permute-done.4
  51.3 1.3 collective-permute-done.5
  53.3 1.5 collective-permute-start.7
  56.0 5.3 %collective-permute-done.6 = f32[64,8,2,128]{3,1,2,0:T(8,128)S(1)} collective-permute-done((f32[64,8,2,128]{3,1,2,0:T(8,128)S(1)}, f32[64,8,2,128]{3,1,2,0:T(8,128)S(1)}, u32[]{:S(2)}, u32[]{:S(2)}) %collective-permute-start.6) | collective-permute-done | bytes 524320 | tf_op jit(solution)/shard_map/ppermute | solution.py:16
  61.3 1.3 collective-permute-done.7
  62.6 7.5 %multiply_subtract_fusion = f32[64,4,8,128]{3,1,2,0:T(4,128)S(1)} fusion(f32[64,4,8,128]{3,1,2,0:T(4,128)S(1)} %get-tuple-element.261, f32[64,4,8,2]{3,1,2,0:T(4,128)S(1)} %get-tuple-element.275, f32[64,4,8,126]{3,1,2,0:T(4,128)S(1)} %get-tuple-element.277, f32[64,4,8,126]{3,1,2,0:T(4,128)S(1)} %get-tuple-element.276, ...), kind=kLoop, calls=%fused_computation.97 | loop fusion | flops 12058624 | bytes 10502144 | tf_op jit(solution)/shard_map/sub | solution.py:79
  70.1 2.1 fusion.17
  72.2 81.9 %psum.7 = f32[64,64]{1,0:T(8,128)S(1)} all-reduce(f32[64,64]{1,0:T(8,128)S(1)} %fusion.17), channel_id=1, replica_groups=mesh['gx'=32,'gy'=8] {'gx','gy'}, use_global_device_ids=true, to_apply=%region_0.1 | all-reduce | flops 4096 | bytes 32768 | tf_op jit(solution)/shard_map/psum | solution.py:87
  154.2 101.3 %while.32 = (s32[]{:T(128)}, f32[64,64]{1,0:T(8,128)S(1)}, f32[64,64]{0,1:T(8,128)S(1)}, s32[]{:T(128)}, s32[]{:T(128)}) while((s32[]{:T(128)}, f32[64,64]{1,0:T(8,128)S(1)}, f32[64,64]{0,1:T(8,128)S(1)}, s32[]{:T(128)}, s32[]{:T(128)}) %tuple.94), condition=%wide.region_3.4_spmd.clone.clone, body=%wide.region_1.3_spmd.clone.clone.sunk | while | flops 62082 | bytes 102112 | solution.py:54
  255.6 95.1 %while.31 = (s32[]{:T(128)}, f32[64,64]{1,0:T(8,128)S(1)}, f32[64,64]{1,0:T(8,128)S(1)}, s32[]{:T(128)}, s32[]{:T(128)}, /*index=5*/s32[]{:T(128)}, s32[]{:T(128)}) while((s32[]{:T(128)}, f32[64,64]{1,0:T(8,128)S(1)}, f32[64,64]{1,0:T(8,128)S(1)}, s32[]{:T(128)}, s32[]{:T(128)}, /*index=5*/s32[]{:T(128)}, s32[]{:T(128)}) %tuple.100), condition=%wide.region_6.7_spmd.clone, body=%wide.region_4.6_spmd.clone.sunk | while | flops 61958 | bytes 67106 | solution.py:73
  256.2 0.8 fusion.75
  257.7 0.8 fusion.75
  259.1 0.8 fusion.75
  262.1 0.8 fusion.75
  263.6 0.8 fusion.75
  265.1 0.8 fusion.75
  266.6 0.8 fusion.75
  268.1 0.8 fusion.75
  271.0 0.8 fusion.75
  272.5 0.8 fusion.75
  274.0 0.8 fusion.75
  275.5 0.8 fusion.75
  350.6 1.6 fusion.16
  352.2 1.2 copy.89
  (601 shorter events, 149.5 us)
Async XLA Ops:
  0.6 5.6 %copy-start = (f32[64,4,8,128]{3,2,1,0:T(8,128)S(1)}, f32[64,4,8,128]{3,2,1,0:T(8,128)}, u32[]{:S(2)}) copy-start(f32[64,4,8,128]{3,2,1,0:T(8,128)} %param.6) | copy-start | bytes 3145732
  3.0 9.8 %collective-permute-start = (f32[64,2,8,128]{3,2,1,0:T(8,128)}, f32[64,2,8,128]{3,2,1,0:T(8,128)S(1)}, u32[]{:S(2)}, u32[]{:S(2)}) collective-permute-start(f32[64,2,8,128]{3,2,1,0:T(8,128)} %get-tuple-element.279), channel_id=1, source_target_pairs={{8,0},{16,8},{24,16},{32,24},{40,32},{48,40},{56,48},{64,56},{72,6... | collective-permute-start | bytes 1572872 | tf_op jit(solution)/shard_map/ppermute | solution.py:16
  6.2 0.7 copy-start.1
  6.2 6.8 %collective-permute-start.1 = (f32[64,2,8,128]{3,2,1,0:T(8,128)}, f32[64,2,8,128]{3,2,1,0:T(8,128)S(1)}, u32[]{:S(2)}, u32[]{:S(2)}) collective-permute-start(f32[64,2,8,128]{3,2,1,0:T(8,128)} %get-tuple-element.278), channel_id=1, source_target_pairs={{0,8},{8,16},{16,24},{24,32},{32,40},{40,48},{48,56},{56,64},{64,7... | collective-permute-start | bytes 1572872 | tf_op jit(solution)/shard_map/ppermute | solution.py:14
  13.7 11.8 %collective-permute-start.2 = (f32[64,8,2,128]{3,1,2,0:T(8,128)S(1)}, f32[64,8,2,128]{3,1,2,0:T(8,128)S(1)}, u32[]{:S(2)}, u32[]{:S(2)}) collective-permute-start(f32[64,8,2,128]{3,1,2,0:T(8,128)S(1)} %get-tuple-element.266), channel_id=1, source_target_pairs={{1,0},{2,1},{3,2},{4,3},{5,4},{6,5},{7,6},{0,7},{9,8},{10,9},{11,1... | collective-permute-start | bytes 1572872 | tf_op jit(solution)/shard_map/ppermute | solution.py:16
  19.3 9.2 %collective-permute-start.3 = (f32[64,8,2,128]{3,1,2,0:T(8,128)S(1)}, f32[64,8,2,128]{3,1,2,0:T(8,128)S(1)}, u32[]{:S(2)}, u32[]{:S(2)}) collective-permute-start(f32[64,8,2,128]{3,1,2,0:T(8,128)S(1)} %get-tuple-element.267), channel_id=1, source_target_pairs={{0,1},{1,2},{2,3},{3,4},{4,5},{5,6},{6,7},{7,0},{8,9},{9,10},{10,1... | collective-permute-start | bytes 1572872 | tf_op jit(solution)/shard_map/ppermute | solution.py:14
  36.4 14.6 %collective-permute-start.4 = (f32[64,2,8,128]{3,2,1,0:T(8,128)S(1)}, f32[64,2,8,128]{3,2,1,0:T(8,128)S(1)}, u32[]{:S(2)}, u32[]{:S(2)}) collective-permute-start(f32[64,2,8,128]{3,2,1,0:T(8,128)S(1)} %copy.74), channel_id=1, source_target_pairs={{8,0},{16,8},{24,16},{32,24},{40,32},{48,40},{56,48},{64,56},{72,6... | collective-permute-start | bytes 1572872 | tf_op jit(solution)/shard_map/ppermute | solution.py:16
  46.2 6.4 %collective-permute-start.5 = (f32[64,2,8,128]{3,2,1,0:T(8,128)S(1)}, f32[64,2,8,128]{3,2,1,0:T(8,128)S(1)}, u32[]{:S(2)}, u32[]{:S(2)}) collective-permute-start(f32[64,2,8,128]{3,2,1,0:T(8,128)S(1)} %copy.76), channel_id=1, source_target_pairs={{0,8},{8,16},{16,24},{24,32},{32,40},{40,48},{48,56},{56,64},{64,7... | collective-permute-start | bytes 1572872 | tf_op jit(solution)/shard_map/ppermute | solution.py:14
  53.2 8.1 %collective-permute-start.6 = (f32[64,8,2,128]{3,1,2,0:T(8,128)S(1)}, f32[64,8,2,128]{3,1,2,0:T(8,128)S(1)}, u32[]{:S(2)}, u32[]{:S(2)}) collective-permute-start(f32[64,8,2,128]{3,1,2,0:T(8,128)S(1)} %get-tuple-element.264), channel_id=1, source_target_pairs={{1,0},{2,1},{3,2},{4,3},{5,4},{6,5},{7,6},{0,7},{9,8},{10,9},{11,1... | collective-permute-start | bytes 1572872 | tf_op jit(solution)/shard_map/ppermute | solution.py:16
  53.3 9.3 %collective-permute-start.7 = (f32[64,8,2,128]{3,1,2,0:T(8,128)S(1)}, f32[64,8,2,128]{3,1,2,0:T(8,128)S(1)}, u32[]{:S(2)}, u32[]{:S(2)}) collective-permute-start(f32[64,8,2,128]{3,1,2,0:T(8,128)S(1)} %get-tuple-element.265), channel_id=1, source_target_pairs={{0,1},{1,2},{2,3},{3,4},{4,5},{5,6},{6,7},{7,0},{8,9},{9,10},{10,1... | collective-permute-start | bytes 1572872 | tf_op jit(solution)/shard_map/ppermute | solution.py:14
  350.6 1.6 copy-start.2
where the time goes:
time: 355 us; the launch traced here: 353 us
  matrix products  103 us (29%)
  blocking collectives  81.9 us (23%)
  other arithmetic  66.1 us (19%)
  loops' own time  46 us (13%)
  waiting for transfers between devices  23.6 us (7%)
  starting transfers between devices  20.4 us (6%)
  local copies, waits for them, and re-layouts  11.1 us (3%)
    psum x1, blocking collectives, shards(): factor = upper_factor(lax.psum(local_gram, ('gx', 'gy')))  81.9 us
    dot_general x64, matrix products, row_step(): jnp.dot(upper_row, inverse, precision=lax.Precision.HIGHEST, preferred_el...  50.1 us
    dot_general x64, matrix products, column_step(): jnp.dot(lower, row_now, precision=lax.Precision.HIGHEST, preferred_elemen...  49.5 us
    another operation x1, loops' own time, upper_factor(): lower = lax.fori_loop(0, order, column_step, jnp.zeros_like(gram))  45.6 us
    reduce_sum x64, other arithmetic, row_step(): pivot = jnp.sum(jnp.where(index == row, upper_row, 0.0))  39.3 us
    ppermute x4, starting transfers between devices, extended(): lax.ppermute(head, axis, [((i + 1) % count, i) for i in range(count)])  18.7 us
    ppermute x4, waiting for transfers between devices, extended(): lax.ppermute(head, axis, [((i + 1) % count, i) for i in range(count)])  17.9 us
    sub x1, other arithmetic, shards(): filtered = 2.0 * (applied - 5.5 * first) / 4.5 - orbitals  7.45 us
  transfers between devices with their start and end apart: 8, of which 7 were waited for; matrix products, arithmetic and copies ran while one was open for 2% of the time, Pallas kernels for 0%

commit v1 on v0

--- a/solution.py
+++ b/solution.py
@@ -84,7 +84,7 @@
         jnp.dot(flat, flat.T, precision=lax.Precision.HIGHEST, preferred_element_type=jnp.float32)
         / cells
     )
-    factor = upper_factor(lax.psum(local_gram, ("gx", "gy")))
+    factor = upper_factor(lax.psum(lax.psum(local_gram, axis_name="gx"), "gy"))
     inverse = upper_inverse(factor)
     solved = jnp.dot(
         inverse.T, flat, precision=lax.Precision.HIGHEST, preferred_element_type=jnp.float32

time: 355 us -> 432 us (1.22)
  the two profiles are of different devices: /device:TPU:1 before, /device:TPU:32 now
where the time goes in v1:
time: 432 us; the launch traced here: 430 us
  blocking collectives  152 us (35%)
  matrix products  103 us (24%)
  other arithmetic  66.1 us (15%)
  loops' own time  46 us (11%)
  waiting for transfers between devices  37.9 us (9%)
  starting transfers between devices  12.9 us (3%)
  local copies, waits for them, and re-layouts  11.1 us (3%)
    psum x2, blocking collectives, shards(): factor = upper_factor(lax.psum(lax.psum(local_gram, axis_name='gx'), 'gy'))  152 us
    dot_general x64, matrix products, row_step(): jnp.dot(upper_row, inverse, precision=lax.Precision.HIGHEST, preferred_el...  50.1 us
    dot_general x64, matrix products, column_step(): jnp.dot(lower, row_now, precision=lax.Precision.HIGHEST, preferred_elemen...  49.5 us
    another operation x1, loops' own time, upper_factor(): lower = lax.fori_loop(0, order, column_step, jnp.zeros_like(gram))  45.6 us
    reduce_sum x64, other arithmetic, row_step(): pivot = jnp.sum(jnp.where(index == row, upper_row, 0.0))  39.3 us
    ppermute x4, waiting for transfers between devices, extended(): lax.ppermute(head, axis, [((i + 1) % count, i) for i in range(count)])  21.4 us
    ppermute x4, waiting for transfers between devices, extended(): lax.ppermute(tail, axis, [(i, (i + 1) % count) for i in range(count)])  16.5 us
    ppermute x4, starting transfers between devices, extended(): lax.ppermute(head, axis, [((i + 1) % count, i) for i in range(count)])  10.7 us
  transfers between devices with their start and end apart: 8, of which 8 were waited for; matrix products, arithmetic and copies ran while one was open for 1% of the time, Pallas kernels for 0%

profile of v1, /device:TPU:32, one launch (start us, length us, event | category | flops | bytes accessed | tf_op | source)
XLA Modules:
  0.0 430.5 jit_solution(14171137369367956073)
XLA Ops:
  0.6 2.3 fusion.60
  3.0 4.6 %collective-permute-start = (f32[64,2,8,128]{3,2,1,0:T(8,128)}, f32[64,2,8,128]{3,2,1,0:T(8,128)S(1)}, u32[]{:S(2)}, u32[]{:S(2)}) collective-permute-start(f32[64,2,8,128]{3,2,1,0:T(8,128)} %get-tuple-element.279), channel_id=1, source_target_pairs={{8,0},{16,8},{24,16},{32,24},{40,32},{48,40},{56,48},{64,56},{72,6... | collective-permute-start | bytes 1572872 | tf_op jit(solution)/shard_map/ppermute | solution.py:16
  9.7 5.0 %collective-permute-done = f32[64,2,8,128]{3,2,1,0:T(8,128)S(1)} collective-permute-done((f32[64,2,8,128]{3,2,1,0:T(8,128)}, f32[64,2,8,128]{3,2,1,0:T(8,128)S(1)}, u32[]{:S(2)}, u32[]{:S(2)}) %collective-permute-start) | collective-permute-done | bytes 524320 | tf_op jit(solution)/shard_map/ppermute | solution.py:16
  14.9 4.8 %collective-permute-done.1 = f32[64,2,8,128]{3,2,1,0:T(8,128)S(1)} collective-permute-done((f32[64,2,8,128]{3,2,1,0:T(8,128)}, f32[64,2,8,128]{3,2,1,0:T(8,128)S(1)}, u32[]{:S(2)}, u32[]{:S(2)}) %collective-permute-start.1) | collective-permute-done | bytes 524320 | tf_op jit(solution)/shard_map/ppermute | solution.py:14
  20.6 1.9 collective-permute-start.3
  23.8 5.9 %collective-permute-done.2 = f32[64,8,2,128]{3,1,2,0:T(8,128)S(1)} collective-permute-done((f32[64,8,2,128]{3,1,2,0:T(8,128)S(1)}, f32[64,8,2,128]{3,1,2,0:T(8,128)S(1)}, u32[]{:S(2)}, u32[]{:S(2)}) %collective-permute-start.2) | collective-permute-done | bytes 524320 | tf_op jit(solution)/shard_map/ppermute | solution.py:16
  29.6 3.9 collective-permute-done.3
  33.6 7.3 %broadcast_multiply_fusion = (f32[64,4,8,128]{3,1,2,0:T(4,128)S(1)}, f32[64,4,8,128]{3,1,2,0:T(4,128)S(1)}) fusion(f32[64,4,8,128]{3,1,2,0:T(4,128)S(1)} %copy.55, f32[4,8,128]{2,0,1:T(4,128)S(1)} %copy.71, f32[64,4,8,2]{3,1,2,0:T(4,128)S(1)} %get-tuple-element.285, f32[64,4,8,126]{3,1,2,0:T(4,128)S(1)} %get-tuple-element.287, ...), kind=kLoop, calls=%fused_computation.105 | loop fusion | flops 11796480 | bytes 9453568 | tf_op jit(solution)/shard_map/div | solution.py:77
  41.4 2.5 collective-permute-start.4
  45.5 5.1 %collective-permute-done.4 = f32[64,2,8,128]{3,2,1,0:T(8,128)S(1)} collective-permute-done((f32[64,2,8,128]{3,2,1,0:T(8,128)S(1)}, f32[64,2,8,128]{3,2,1,0:T(8,128)S(1)}, u32[]{:S(2)}, u32[]{:S(2)}) %collective-permute-start.4) | collective-permute-done | bytes 524320 | tf_op jit(solution)/shard_map/ppermute | solution.py:16
  50.9 5.2 %collective-permute-done.5 = f32[64,2,8,128]{3,2,1,0:T(8,128)S(1)} collective-permute-done((f32[64,2,8,128]{3,2,1,0:T(8,128)S(1)}, f32[64,2,8,128]{3,2,1,0:T(8,128)S(1)}, u32[]{:S(2)}, u32[]{:S(2)}) %collective-permute-start.5) | collective-permute-done | bytes 524320 | tf_op jit(solution)/shard_map/ppermute | solution.py:14
  56.8 3.3 collective-permute-start.6
  61.4 5.4 %collective-permute-done.6 = f32[64,8,2,128]{3,1,2,0:T(8,128)S(1)} collective-permute-done((f32[64,8,2,128]{3,1,2,0:T(8,128)S(1)}, f32[64,8,2,128]{3,1,2,0:T(8,128)S(1)}, u32[]{:S(2)}, u32[]{:S(2)}) %collective-permute-start.6) | collective-permute-done | bytes 524320 | tf_op jit(solution)/shard_map/ppermute | solution.py:16
  66.8 2.5 collective-permute-done.7
  69.3 7.5 %multiply_subtract_fusion = f32[64,4,8,128]{3,1,2,0:T(4,128)S(1)} fusion(f32[64,4,8,128]{3,1,2,0:T(4,128)S(1)} %get-tuple-element.261, f32[64,4,8,2]{3,1,2,0:T(4,128)S(1)} %get-tuple-element.275, f32[64,4,8,126]{3,1,2,0:T(4,128)S(1)} %get-tuple-element.277, f32[64,4,8,126]{3,1,2,0:T(4,128)S(1)} %get-tuple-element.276, ...), kind=kLoop, calls=%fused_computation.97 | loop fusion | flops 12058624 | bytes 10502144 | tf_op jit(solution)/shard_map/sub | solution.py:79
  76.8 2.1 fusion.17
  78.9 124.7 %psum.14 = f32[64,64]{1,0:T(8,128)S(1)} all-reduce(f32[64,64]{1,0:T(8,128)S(1)} %fusion.17), channel_id=1, replica_groups=mesh['gx'=32,'gy'=8] {'gx'}, use_global_device_ids=true, to_apply=%region_0.1 | all-reduce | flops 4096 | bytes 32768 | tf_op jit(solution)/shard_map/psum | solution.py:87
  203.6 27.5 %psum.15 = f32[64,64]{1,0:T(8,128)S(1)} all-reduce(f32[64,64]{1,0:T(8,128)S(1)} %psum.14), channel_id=1, replica_groups=mesh['gx'=32,'gy'=8] {'gy'}, use_global_device_ids=true, to_apply=%region_1.2 | all-reduce | flops 4096 | bytes 32768 | tf_op jit(solution)/shard_map/psum | solution.py:87
  231.2 101.3 %while.32 = (s32[]{:T(128)}, f32[64,64]{1,0:T(8,128)S(1)}, f32[64,64]{0,1:T(8,128)S(1)}, s32[]{:T(128)}, s32[]{:T(128)}) while((s32[]{:T(128)}, f32[64,64]{1,0:T(8,128)S(1)}, f32[64,64]{0,1:T(8,128)S(1)}, s32[]{:T(128)}, s32[]{:T(128)}) %tuple.94), condition=%wide.region_4.5_spmd.clone.clone, body=%wide.region_2.4_spmd.clone.clone.sunk | while | flops 62082 | bytes 102112 | solution.py:54
  332.6 95.1 %while.31 = (s32[]{:T(128)}, f32[64,64]{1,0:T(8,128)S(1)}, f32[64,64]{1,0:T(8,128)S(1)}, s32[]{:T(128)}, s32[]{:T(128)}, /*index=5*/s32[]{:T(128)}, s32[]{:T(128)}) while((s32[]{:T(128)}, f32[64,64]{1,0:T(8,128)S(1)}, f32[64,64]{1,0:T(8,128)S(1)}, s32[]{:T(128)}, s32[]{:T(128)}, /*index=5*/s32[]{:T(128)}, s32[]{:T(128)}) %tuple.100), condition=%wide.region_7.8_spmd.clone, body=%wide.region_5.7_spmd.clone.sunk | while | flops 61958 | bytes 67106 | solution.py:73
  333.2 0.8 fusion.75
  334.7 0.8 fusion.75
  336.2 0.8 fusion.75
  337.7 0.8 fusion.75
  339.2 0.8 fusion.75
  340.6 0.8 fusion.75
  342.1 0.8 fusion.75
  343.6 0.8 fusion.75
  345.1 0.8 fusion.75
  346.6 0.8 fusion.75
  427.7 1.6 fusion.16
  429.3 1.2 copy.89
  (602 shorter events, 151.2 us)
Async XLA Ops:
  0.6 7.0 %copy-start = (f32[64,4,8,128]{3,2,1,0:T(8,128)S(1)}, f32[64,4,8,128]{3,2,1,0:T(8,128)}, u32[]{:S(2)}) copy-start(f32[64,4,8,128]{3,2,1,0:T(8,128)} %param.6) | copy-start | bytes 3145732
  3.0 11.7 %collective-permute-start = (f32[64,2,8,128]{3,2,1,0:T(8,128)}, f32[64,2,8,128]{3,2,1,0:T(8,128)S(1)}, u32[]{:S(2)}, u32[]{:S(2)}) collective-permute-start(f32[64,2,8,128]{3,2,1,0:T(8,128)} %get-tuple-element.279), channel_id=1, source_target_pairs={{8,0},{16,8},{24,16},{32,24},{40,32},{48,40},{56,48},{64,56},{72,6... | collective-permute-start | bytes 1572872 | tf_op jit(solution)/shard_map/ppermute | solution.py:16
  7.6 0.7 copy-start.1
  7.6 12.1 %collective-permute-start.1 = (f32[64,2,8,128]{3,2,1,0:T(8,128)}, f32[64,2,8,128]{3,2,1,0:T(8,128)S(1)}, u32[]{:S(2)}, u32[]{:S(2)}) collective-permute-start(f32[64,2,8,128]{3,2,1,0:T(8,128)} %get-tuple-element.278), channel_id=1, source_target_pairs={{0,8},{8,16},{16,24},{24,32},{32,40},{40,48},{48,56},{56,64},{64,7... | collective-permute-start | bytes 1572872 | tf_op jit(solution)/shard_map/ppermute | solution.py:14
  20.4 9.3 %collective-permute-start.2 = (f32[64,8,2,128]{3,1,2,0:T(8,128)S(1)}, f32[64,8,2,128]{3,1,2,0:T(8,128)S(1)}, u32[]{:S(2)}, u32[]{:S(2)}) collective-permute-start(f32[64,8,2,128]{3,1,2,0:T(8,128)S(1)} %get-tuple-element.266), channel_id=1, source_target_pairs={{1,0},{2,1},{3,2},{4,3},{5,4},{6,5},{7,6},{0,7},{9,8},{10,9},{11,1... | collective-permute-start | bytes 1572872 | tf_op jit(solution)/shard_map/ppermute | solution.py:16
  20.6 13.0 %collective-permute-start.3 = (f32[64,8,2,128]{3,1,2,0:T(8,128)S(1)}, f32[64,8,2,128]{3,1,2,0:T(8,128)S(1)}, u32[]{:S(2)}, u32[]{:S(2)}) collective-permute-start(f32[64,8,2,128]{3,1,2,0:T(8,128)S(1)} %get-tuple-element.267), channel_id=1, source_target_pairs={{0,1},{1,2},{2,3},{3,4},{4,5},{5,6},{6,7},{7,0},{8,9},{9,10},{10,1... | collective-permute-start | bytes 1572872 | tf_op jit(solution)/shard_map/ppermute | solution.py:14
  41.4 9.2 %collective-permute-start.4 = (f32[64,2,8,128]{3,2,1,0:T(8,128)S(1)}, f32[64,2,8,128]{3,2,1,0:T(8,128)S(1)}, u32[]{:S(2)}, u32[]{:S(2)}) collective-permute-start(f32[64,2,8,128]{3,2,1,0:T(8,128)S(1)} %copy.74), channel_id=1, source_target_pairs={{8,0},{16,8},{24,16},{32,24},{40,32},{48,40},{56,48},{64,56},{72,6... | collective-permute-start | bytes 1572872 | tf_op jit(solution)/shard_map/ppermute | solution.py:16
  44.0 12.2 %collective-permute-start.5 = (f32[64,2,8,128]{3,2,1,0:T(8,128)S(1)}, f32[64,2,8,128]{3,2,1,0:T(8,128)S(1)}, u32[]{:S(2)}, u32[]{:S(2)}) collective-permute-start(f32[64,2,8,128]{3,2,1,0:T(8,128)S(1)} %copy.76), channel_id=1, source_target_pairs={{0,8},{8,16},{16,24},{24,32},{32,40},{40,48},{48,56},{56,64},{64,7... | collective-permute-start | bytes 1572872 | tf_op jit(solution)/shard_map/ppermute | solution.py:14
  56.8 10.0 %collective-permute-start.6 = (f32[64,8,2,128]{3,1,2,0:T(8,128)S(1)}, f32[64,8,2,128]{3,1,2,0:T(8,128)S(1)}, u32[]{:S(2)}, u32[]{:S(2)}) collective-permute-start(f32[64,8,2,128]{3,1,2,0:T(8,128)S(1)} %get-tuple-element.264), channel_id=1, source_target_pairs={{1,0},{2,1},{3,2},{4,3},{5,4},{6,5},{7,6},{0,7},{9,8},{10,9},{11,1... | collective-permute-start | bytes 1572872 | tf_op jit(solution)/shard_map/ppermute | solution.py:16
  60.1 9.2 %collective-permute-start.7 = (f32[64,8,2,128]{3,1,2,0:T(8,128)S(1)}, f32[64,8,2,128]{3,1,2,0:T(8,128)S(1)}, u32[]{:S(2)}, u32[]{:S(2)}) collective-permute-start(f32[64,8,2,128]{3,1,2,0:T(8,128)S(1)} %get-tuple-element.265), channel_id=1, source_target_pairs={{0,1},{1,2},{2,3},{3,4},{4,5},{5,6},{6,7},{7,0},{8,9},{9,10},{10,1... | collective-permute-start | bytes 1572872 | tf_op jit(solution)/shard_map/ppermute | solution.py:14
  427.7 1.6 copy-start.2
